TPU v7x, 256 devices: a whole 4x4x8 slice. The times are simulated.
256 devices in a mesh: dp: 32 (over x, y, core), shard: 8 (over z).
Axes of the slice: x: 4, y: 4, z: 8, core: 2. Of those that a mesh axis runs over, the one named last changes fastest.
Arguments:
- audio: bfloat16 [65536, 512], P(('dp', 'shard')), may hold values from -6 to 6
- cotangent: bfloat16 [65536, 512], P(('dp', 'shard')), may hold values from -6 to 6
- clip_lengths: int32 [256, 8], P(('dp', 'shard')), may hold values from 1 to 128, 256 in all within a row
- conv_weight: bfloat16 [3584, 512], P('shard'), may hold values from -0.09375 to 0.09375
- mix_weight: bfloat16 [512, 512], P('shard'), may hold values from -0.25 to 0.25
- conv_bias: float32 [512], replicated, may hold values from -3 to 3
- alpha_in: float32 [512], replicated, may hold values from 0.5 to 3
- alpha_mid: float32 [512], replicated, may hold values from 0.5 to 3
Outputs:
- in_grad: bfloat16 [65536, 512], P(('dp', 'shard'))
- conv_grad: float32 [3584, 512], P(('dp', 'shard'))
- mix_grad: float32 [512, 512], P(('dp', 'shard'))
- vector_grad: float32 [4, 512], P(None, ('dp', 'shard'))
Inputs may be any that keep to these rules, and one draw needn't show every extreme that they name: `clip_lengths`: each device's clip lengths sum to 256; the largest on each device is 128.
All inputs are finite; a program needn't handle non-finite values.
Results may differ from a plain program's by a relative error of at most 0.01.
Values may be sent and summed in bfloat16 or wider, within the bound.
No kernel may reach another device: no remote copies, remote signals or barrier semaphores. Data moves between devices by JAX's collectives and lax.ppermute only.
A program may use at most 64 MiB of HBM per device.

v0:
```python
import jax
import jax.numpy as jnp
from jax import lax
from jax.sharding import Mesh, PartitionSpec as P

C = 512
TAPS = 7
DILATION_SIZE = 9
FRAME_AXES = ("x", "y", "c", "z")
SCATTER_ORDER = ("c", "z", "y", "x")
EXTRA_COLUMNS = 128


def shift_rows(block, tap_offset, fill):
    rows = block.shape[0]
    shift_amount = min(abs(tap_offset), rows)
    if shift_amount == 0:
        return block
    edge_padding = jnp.full((shift_amount,) + block.shape[1:], fill, block.dtype)
    if tap_offset > 0:
        return jnp.concatenate([block[shift_amount:], edge_padding], axis=0)
    return jnp.concatenate([edge_padding, block[: rows - shift_amount]], axis=0)


def clip_masks(lengths_row, rows):
    clip_ends = jnp.cumsum(lengths_row)
    position = jnp.arange(rows, dtype=jnp.int32)
    clip_id = jnp.sum((position[:, None] >= clip_ends[None, :]).astype(jnp.int32), axis=1)
    result = []
    for kernel_tap_index in range(TAPS):
        tap_offset = (kernel_tap_index - 3) * DILATION_SIZE
        result.append(shift_rows(clip_id, tap_offset, -1) == clip_id)
    return result


def snake_parts(value, alpha):
    sine = jnp.sin(alpha * value)
    double = jnp.sin(2.0 * alpha * value)
    return (
        value + sine * sine / alpha,
        1.0 + double,
        value * double / alpha - sine * sine / (alpha * alpha),
    )


def permute_scatter(value, axis):
    n = lax.axis_size(axis)
    me = lax.axis_index(axis)
    each = value.shape[0] // n
    total = lax.dynamic_slice_in_dim(value, me * each, each)
    for step in range(1, n):
        chunk = lax.dynamic_slice_in_dim(value, (me + step) % n * each, each)
        total = total + lax.ppermute(chunk, axis, [(j, (j + step) % n) for j in range(n)])
    return total


def per_device(
    audio, cotangent, clip_lengths, conv_weight, mix_weight, conv_bias, alpha_in, alpha_mid
):
    rows = audio.shape[0]
    same_clip_flags = clip_masks(clip_lengths[0], rows)
    conv_rows = conv_weight.shape[0]
    mix_rows = mix_weight.shape[0]
    both = jnp.concatenate([conv_weight, mix_weight], axis=0)
    core = lax.axis_index("c")
    half = C // 2
    own = lax.all_gather(
        lax.dynamic_slice_in_dim(both, core * half, half, axis=1), "z", axis=0, tiled=True
    )
    audio_f = audio.astype(jnp.float32)
    act_in, slope_in, dalpha_in = snake_parts(audio_f, alpha_in)
    first = act_in.astype(jnp.bfloat16)
    columns = []
    for kernel_tap_index in range(TAPS):
        tap_offset = (kernel_tap_index - 3) * DILATION_SIZE
        moved = shift_rows(first, tap_offset, 0)
        columns.append(
            jnp.where(same_clip_flags[kernel_tap_index][:, None], moved, jnp.zeros_like(moved))
        )
    unfolded = jnp.concatenate(columns, axis=1)
    sizes = [lax.axis_size(a) for a in FRAME_AXES]
    devices = 1
    for s in sizes:
        devices *= s
    conv_each = unfolded.shape[1] // devices
    mix_each = C // devices
    order = [FRAME_AXES.index(a) for a in SCATTER_ORDER]

    def lay_out(left):
        left = jnp.concatenate(left, axis=2).reshape(rows, *sizes, conv_each + mix_each)
        return left.transpose(0, *[o + 1 for o in order], 5).reshape(rows, -1)

    conv_lhs = lay_out(
        [
            unfolded.reshape(rows, devices, conv_each),
            jnp.zeros((rows, devices, mix_each), unfolded.dtype),
        ]
    )
    own, conv_lhs = lax.optimization_barrier((own, conv_lhs))
    other = lax.ppermute(own, "c", [(0, 1), (1, 0)])
    first_half = jnp.where(core == 0, own, other)
    second_half = jnp.where(core == 0, other, own)
    gathered = jnp.concatenate([first_half, second_half], axis=1)
    gathered = gathered.reshape(-1, conv_rows + mix_rows, C)
    conv_full = gathered[:, :conv_rows].reshape(-1, C)
    mix_full = gathered[:, conv_rows:].reshape(-1, C)
    product = jnp.dot(unfolded, conv_full, preferred_element_type=jnp.float32)
    pre = product + conv_bias
    act_mid, slope_mid, dalpha_mid = snake_parts(pre, alpha_mid)
    second = act_mid.astype(jnp.bfloat16)
    second_gradient = lax.dot_general(
        cotangent, mix_full, (((1,), (1,)), ((), ())), preferred_element_type=jnp.float32
    )
    d_pre = (second_gradient * slope_mid).astype(jnp.bfloat16)
    d_unf = lax.dot_general(
        d_pre, conv_full, (((1,), (1,)), ((), ())), preferred_element_type=jnp.float32
    ).astype(jnp.bfloat16)
    d_first = jnp.zeros((rows, C), jnp.float32)
    for kernel_tap_index in range(TAPS):
        tap_offset = (kernel_tap_index - 3) * DILATION_SIZE
        piece = d_unf[:, kernel_tap_index * C : (kernel_tap_index + 1) * C].astype(jnp.float32)
        piece = jnp.where(same_clip_flags[kernel_tap_index][:, None], piece, jnp.zeros_like(piece))
        d_first = d_first + shift_rows(piece, -tap_offset, 0.0)
    in_grad = (cotangent.astype(jnp.float32) + d_first * slope_in).astype(jnp.bfloat16)
    vectors = jnp.stack(
        [
            jnp.sum(d_pre.astype(jnp.float32), axis=0),
            jnp.sum(cotangent.astype(jnp.float32), axis=0),
            jnp.sum(d_first * dalpha_in, axis=0),
            jnp.sum(second_gradient * dalpha_mid, axis=0),
        ]
    )
    mix_lhs = lay_out(
        [
            jnp.zeros((rows, devices, conv_each), second.dtype),
            second.reshape(rows, devices, mix_each),
        ]
    )
    packed = lax.dot_general(
        jnp.concatenate([conv_lhs, mix_lhs], axis=0),
        jnp.concatenate([d_pre, cotangent], axis=0),
        (((0,), (0,)), ((), ())),
        preferred_element_type=jnp.float32,
    )
    first_axis, second_axis, *rest = SCATTER_ORDER
    packed = lax.psum_scatter(
        packed.astype(jnp.bfloat16), first_axis, scatter_dimension=0, tiled=True
    )
    vectors = lax.psum(vectors, first_axis)
    packed, vectors = lax.optimization_barrier((packed, vectors))
    packed = lax.psum_scatter(packed, second_axis, scatter_dimension=0, tiled=True)
    packed = packed.astype(jnp.float32)
    vectors = lax.psum(vectors, second_axis)
    block = conv_each + mix_each
    held = packed.shape[0] // block
    share = vectors.shape[1] // devices
    vec_blocks = vectors.reshape(4, devices, share).transpose(1, 0, 2).reshape(*sizes, 4 * share)
    kept_names = list(FRAME_AXES)
    for axis in (first_axis, second_axis):
        position = kept_names.index(axis)
        vec_blocks = jnp.take(vec_blocks, lax.axis_index(axis), axis=position)
        kept_names.pop(position)
    vec_blocks = vec_blocks.transpose(*[kept_names.index(a) for a in rest], len(kept_names))
    vec_blocks = vec_blocks.reshape(held, 4 * share)
    extra = jnp.zeros((held, block, EXTRA_COLUMNS), jnp.float32)
    extra = extra.at[:, 0, : 4 * share].set(vec_blocks)
    packed = jnp.concatenate([packed.reshape(held, block, C), extra], axis=2)
    packed = packed.reshape(held * block, C + EXTRA_COLUMNS)
    for axis in rest:
        packed = permute_scatter(packed, axis)
    conv_grad = packed[:conv_each, :C]
    mix_grad = packed[conv_each:, :C]
    vector_grad = packed[0, C : C + 4 * share].reshape(4, share)
    return (in_grad, conv_grad, mix_grad, vector_grad)


def solution(mesh):
    devices = mesh.devices
    xs = len({d.coords[0] for d in devices.flat})
    ys = len({d.coords[1] for d in devices.flat})
    dp, shard = devices.shape
    split = Mesh(devices.reshape(xs, ys, dp // (xs * ys), shard), FRAME_AXES)
    frames = P(FRAME_AXES)
    placed = (frames, frames, frames, P("z", None), P("z", None), P(), P(), P())
    return jax.shard_map(
        per_device,
        mesh=split,
        in_specs=placed,
        out_specs=(frames, frames, frames, P(None, FRAME_AXES)),
        check_vma=False,
    )
```

profile of v0, /device:TPU:8, one launch (start us, length us, event | category | flops | bytes accessed | tf_op | source)
XLA Modules:
  0.0 164.8 jit_solution(2630460605486601233)
XLA Ops:
  7.2 1.7 %fusion.19 = bf16[512,256]{1,0:T(8,128)(2,1)} fusion(s32[]{:T(128)S(6)} %select_n.127, bf16[448,512]{1,0:T(8,128)(2,1)} %param.13, bf16[64,512]{1,0:T(8,128)(2,1)} %param.14), kind=kLoop, calls=%fused_computation.55 | loop fusion | flops 524288 | bytes 786436 | tf_op jit(solution)/shard_map/concatenate | solution.py:64
  9.0 0.8 reduce-window.8
  10.2 2.8 %fusion.10 = bf16[256,512]{1,0:T(8,128)(2,1)S(1)} fusion(bf16[256,512]{1,0:T(8,128)(2,1)} %param.10, f32[512]{0:T(512)} %param.16), kind=kLoop, calls=%fused_computation.31 | loop fusion | flops 786432 | bytes 526336 | tf_op jit(solution)/shard_map/convert_element_type | solution.py:72
  13.9 1.8 %constant_dynamic-update-slice_fusion = bf16[256,3584]{1,0:T(8,128)(2,1)S(1)} fusion(bf16[256,3584]{1,0:T(8,128)(2,1)S(1)} %select_dynamic-update-slice_fusion.3, f32[512]{0:T(512)S(1)} %copy-done.5, bf16[256,512]{1,0:T(8,128)(2,1)S(1)} %copy-done.1), kind=kLoop, calls=%fused_computation.72 | loop fusion | flops 786432 | bytes 526336
  16.1 1.3 copy-done.2
  17.4 2.3 %copy.34 = bf16[256,3584]{0,1:T(8,128)(2,1)} copy(bf16[256,3584]{1,0:T(8,128)(2,1)S(1)} %select_dynamic-update-slice_fusion) | data formatting | bytes 3670016 | tf_op jit(solution)/shard_map/concatenate | solution.py:80
  19.7 2.5 %reshape.128 = bf16[256,256,14]{0,2,1:T(8,128)(2,1)S(1)} reshape(bf16[256,3584]{0,1:T(8,128)(2,1)} %copy.34) | data formatting | bytes 3670016 | tf_op jit(solution)/shard_map/reshape | solution.py:95
  22.8 31.3 %all-gather.2.cloned.1.call-done = bf16[4096,256]{1,0:T(8,128)(2,1)} async-done(((bf16[512,256]{1,0:T(8,128)(2,1)}), bf16[4096,256]{1,0:T(8,128)(2,1)}) %all-gather.2.cloned.1.call-update) | async-done | bytes 2097168 | tf_op jit(solution)/shard_map/all_gather | solution.py:67
  54.1 4.5 %collective-permute-done = bf16[4096,256]{1,0:T(8,128)(2,1)} collective-permute-done((bf16[4096,256]{1,0:T(8,128)(2,1)}, bf16[4096,256]{1,0:T(8,128)(2,1)}, u32[]{:S(2)}, u32[]{:S(2)}) %collective-permute-start) | collective-permute-done | bytes 2097184 | tf_op jit(solution)/shard_map/ppermute | solution.py:100
  58.6 2.5 %broadcast_select_fusion.1 = (bf16[4096,256]{1,0:T(8,128)(2,1)S(1)}, bf16[4096,256]{1,0:T(8,128)(2,1)S(1)}) fusion(bf16[4096,256]{1,0:T(8,128)(2,1)} %all-gather.2.cloned.1.call-done, bf16[4096,256]{1,0:T(8,128)(2,1)} %collective-permute-done, pred[]{:T(512)S(6)} %eq.30), kind=kLoop, calls=%fused_computation.7 | loop fusion | flops 2097152 | bytes 8388609 | tf_op jit(solution)/shard_map/jit(_where)/select_n | solution.py:101
  61.8 1.8 %copy-done.3 = bf16[256,3584]{1,0:T(8,128)(2,1)S(1)} copy-done((bf16[256,3584]{1,0:T(8,128)(2,1)S(1)}, bf16[256,3584]{1,0:T(8,128)(2,1)}, u32[]{:S(2)}) %copy-start.3) | copy-done | bytes 1835032
  63.6 1.1 convolution_add_fusion
  64.7 4.1 %convert_reduce_fusion.1 = (f32[512]{0:T(512)S(1)}, bf16[256,512]{1,0:T(8,128)(2,1)S(1)}, f32[512]{0:T(512)S(1)}, bf16[256,512]{1,0:T(8,128)(2,1)S(1)}) fusion(f32[256,512]{1,0:T(8,128)S(1)} %convolution_add_fusion, f32[512]{0:T(512)S(1)} %get-tuple-element.90, f32[512]{0:T(512)S(1)} %get-tuple-element.91, f32[512]{0:T(512)S(1)} %copy-done.6, ...), kind=kOutput, calls=%fused_computation.42 | convolution fusion | flops 136444928 | bytes 1845248 | tf_op jit(solution)/shard_map/dot_general | solution.py:111
  69.8 4.4 %convolution_convert_fusion = bf16[4096,512]{1,0:T(8,128)(2,1)} fusion(bf16[256,4096]{0,1:T(8,128)(2,1)S(1)} %bitcast.52, bf16[256,4096]{0,1:T(8,128)(2,1)S(1)} %bitcast.51, bf16[256,512]{1,0:T(8,128)(2,1)S(1)} %copy-done.4, bf16[256,512]{1,0:T(8,128)(2,1)S(1)} %get-tuple-element.63), kind=kOutput, calls=%fused_computation | convolution fusion | flops 2159017984 | bytes 8912896 | tf_op jit(solution)/shard_map/dot_general | solution.py:139
  74.7 3.2 %convolution_convert_fusion.1 = bf16[256,3584]{1,0:T(8,128)(2,1)S(1)} fusion(bf16[256,512]{1,0:T(8,128)(2,1)S(1)} %get-tuple-element.63, bf16[3584,512]{1,0:T(8,128)(2,1)} %bitcast.48), kind=kOutput, calls=%fused_computation.1 | convolution fusion | flops 940441600 | bytes 5767168 | tf_op jit(solution)/shard_map/dot_general | solution.py:115
  78.6 3.9 %fusion.18 = (f32[512]{0:T(512)S(1)}, f32[256,512]{1,0:T(8,128)S(1)}) fusion(bf16[256,512]{1,0:T(8,128)(2,1)S(1)} %copy-done.1, f32[512]{0:T(512)S(1)} %get-tuple-element.93, f32[512]{0:T(512)S(1)} %get-tuple-element.92, f32[512]{0:T(512)S(1)} %copy-done.5, f32[229,512]{1,0:T(8,128)S(1)} %get-tuple-element.110, f32[238,512]{1,0:T(8,128)S(1)} %get-tuple-element.108, ...), kind=kLoop, calls=%fused_computation.48 | loop fusion | flops 2227712 | bytes 3981312 | tf_op jit(solution)/shard_map/reduce_sum | solution.py:129
  82.5 2.5 %convert_reduce_fusion = (f32[512]{0:T(512)S(1)}, bf16[256,512]{1,0:T(8,128)(2,1)}) fusion(bf16[256,512]{1,0:T(8,128)(2,1)S(1)} %copy-done.4, f32[256,512]{1,0:T(8,128)S(1)} %get-tuple-element.65, bf16[256,512]{1,0:T(8,128)(2,1)S(1)} %copy-done.1, f32[512]{0:T(512)S(1)} %get-tuple-element.92), kind=kLoop, calls=%fused_computation.22 | loop fusion | flops 1048064 | bytes 1314816 | tf_op jit(solution)/shard_map/reduce_sum | solution.py:128
  85.0 2.5 %psum.14 = f32[4,512]{1,0:T(4,128)S(1)} all-reduce(f32[4,512]{1,0:T(4,128)S(1)} %pad_maximum_fusion.1), channel_id=1, replica_groups=mesh['x'=4,'y'=4,'c'=2,'z'=8] {'c'}, use_global_device_ids=true, to_apply=%region_7.8 | all-reduce | flops 2048 | bytes 16384 | tf_op jit(solution)/shard_map/psum | solution.py:149
  87.5 2.9 %reduce-scatter.3.cloned.1.call-done = bf16[2048,512]{1,0:T(8,128)(2,1)} async-done(((bf16[4096,512]{1,0:T(8,128)(2,1)}), bf16[2048,512]{1,0:T(8,128)(2,1)}) %reduce-scatter.3.cloned.1.call-update) | async-done | bytes 2097168 | tf_op jit(solution)/shard_map/reduce_scatter | solution.py:146
  91.0 32.0 %psum.15 = f32[4,4,2,8,8]{3,2,1,0,4:T(2,128)S(1)} all-reduce(f32[4,4,2,8,8]{3,2,1,0,4:T(2,128)S(1)} %reshape.138), channel_id=1, replica_groups=mesh['x'=4,'y'=4,'c'=2,'z'=8] {'z'}, use_global_device_ids=true, to_apply=%region_9.10 | all-reduce | flops 2048 | bytes 16384 | tf_op jit(solution)/shard_map/psum | solution.py:153
  123.4 13.6 %reduce-scatter.5.cloned.1.call-done = bf16[256,512]{1,0:T(8,128)(2,1)} async-done(((bf16[2048,512]{1,0:T(8,128)(2,1)}), bf16[256,512]{1,0:T(8,128)(2,1)}) %reduce-scatter.5.cloned.1.call-update) | async-done | bytes 262160 | tf_op jit(solution)/shard_map/reduce_scatter | solution.py:151
  137.0 1.0 convert_element_type.72
  138.0 1.6 collective-permute-start.1
  139.6 1.5 collective-permute-start.2
  141.1 2.3 %collective-permute-start.3 = (f32[64,640]{1,0:T(8,128)S(1)}, f32[64,640]{1,0:T(8,128)S(1)}, u32[]{:S(2)}, u32[]{:S(2)}) collective-permute-start(f32[64,640]{1,0:T(8,128)S(1)} %get-tuple-element.77), channel_id=1, source_target_pairs={{0,48},{16,0},{32,16},{48,32},{1,49},{17,1},{33,17},{49,33},{2,50}... | collective-permute-start | bytes 491528 | tf_op jit(solution)/shard_map/ppermute | solution.py:53
  143.4 3.1 %collective-permute-done.2 = f32[64,640]{1,0:T(8,128)S(1)} collective-permute-done((f32[64,640]{1,0:T(8,128)S(1)}, f32[64,640]{1,0:T(8,128)S(1)}, u32[]{:S(2)}, u32[]{:S(2)}) %collective-permute-start.2) | collective-permute-done | bytes 163872 | tf_op jit(solution)/shard_map/ppermute | solution.py:53
  146.5 1.6 collective-permute-done.3
  148.2 1.2 collective-permute-start.4
  149.4 2.9 %collective-permute-start.5 = (f32[16,640]{1,0:T(8,128)S(1)}, f32[16,640]{1,0:T(8,128)S(1)}, u32[]{:S(2)}, u32[]{:S(2)}) collective-permute-start(f32[16,640]{1,0:T(8,128)S(1)} %get-tuple-element.89), channel_id=1, source_target_pairs={{0,128},{64,192},{128,0},{192,64},{1,129},{65,193},{129,1},{193,65... | collective-permute-start | bytes 122888 | tf_op jit(solution)/shard_map/ppermute | solution.py:53
  152.2 1.3 collective-permute-start.6
  153.5 1.3 collective-permute-done.5
  154.9 1.4 collective-permute-done.6
  (71 shorter events, 8.0 us)
Async XLA Ops:
  7.2 46.9 %all-gather.2.cloned.1.call-start = ((), (), s32[]{:S(2)}) async-start(), calls=%async_computation.2 | async-start | bytes 2359296 | tf_op jit(solution)/shard_map/all_gather | solution.py:67
  8.9 81.5 %reduce-scatter.3.cloned.1.call-start = ((), (), s32[]{:S(2)}) async-start(), calls=%async_computation.3 | async-start | bytes 6291456 | tf_op jit(solution)/shard_map/reduce_scatter | solution.py:146
  12.9 1.0 copy-start.1
  12.9 0.9 copy-start.5
  16.1 1.3 copy-start.2
  22.5 31.7 %copy-start.6 = (f32[512]{0:T(512)S(1)}, f32[512]{0:T(512)}, u32[]{:S(2)}) copy-start(f32[512]{0:T(512)} %param.17) | copy-start | bytes 6148
  54.1 4.5 %collective-permute-start = (bf16[4096,256]{1,0:T(8,128)(2,1)}, bf16[4096,256]{1,0:T(8,128)(2,1)}, u32[]{:S(2)}, u32[]{:S(2)}) collective-permute-start(bf16[4096,256]{1,0:T(8,128)(2,1)} %all-gather.2.cloned.1.call-done), channel_id=1, source_target_pairs={{0,8},{8,0},{1,9},{9,1},{2,10},{10,2},{3,11},{11,3},{4,12},{12,4},... | collective-permute-start | bytes 6291464 | tf_op jit(solution)/shard_map/ppermute | solution.py:100
  61.4 2.2 %copy-start.3 = (bf16[256,3584]{1,0:T(8,128)(2,1)S(1)}, bf16[256,3584]{1,0:T(8,128)(2,1)}, u32[]{:S(2)}) copy-start(bf16[256,3584]{1,0:T(8,128)(2,1)} %copy-done.2) | copy-start | bytes 5505028
  61.5 2.2 %copy-start.7 = (f32[512]{0:T(512)S(1)}, f32[512]{0:T(512)}, u32[]{:S(2)}) copy-start(f32[512]{0:T(512)} %param.15) | copy-start | bytes 6148
  61.7 3.0 %copy-start = (bf16[8,448,512]{2,1,0:T(8,128)(2,1)}, bf16[8,448,512]{2,1,0:T(8,128)(2,1)S(1)}, u32[]{:S(2)}) copy-start(bf16[8,448,512]{2,1,0:T(8,128)(2,1)S(1)} %slice.174) | copy-start | bytes 11010052
  63.6 1.1 copy-start.4
  74.2 62.7 %reduce-scatter.5.cloned.1.call-start = ((), (), s32[]{:S(2)}) async-start(), calls=%async_computation.4 | async-start | bytes 2359296 | tf_op jit(solution)/shard_map/reduce_scatter | solution.py:151
  138.0 5.4 %collective-permute-start.1 = (f32[64,640]{1,0:T(8,128)S(1)}, f32[64,640]{1,0:T(8,128)S(1)}, u32[]{:S(2)}, u32[]{:S(2)}) collective-permute-start(f32[64,640]{1,0:T(8,128)S(1)} %get-tuple-element.75), channel_id=1, source_target_pairs={{0,16},{16,32},{32,48},{48,0},{1,17},{17,33},{33,49},{49,1},{2,18}... | collective-permute-start | bytes 491528 | tf_op jit(solution)/shard_map/ppermute | solution.py:53
  139.6 6.9 %collective-permute-start.2 = (f32[64,640]{1,0:T(8,128)S(1)}, f32[64,640]{1,0:T(8,128)S(1)}, u32[]{:S(2)}, u32[]{:S(2)}) collective-permute-start(f32[64,640]{1,0:T(8,128)S(1)} %get-tuple-element.76), channel_id=1, source_target_pairs={{0,32},{16,48},{32,0},{48,16},{1,33},{17,49},{33,1},{49,17},{2,34}... | collective-permute-start | bytes 491528 | tf_op jit(solution)/shard_map/ppermute | solution.py:53
  141.1 7.1 %collective-permute-start.3 = (f32[64,640]{1,0:T(8,128)S(1)}, f32[64,640]{1,0:T(8,128)S(1)}, u32[]{:S(2)}, u32[]{:S(2)}) collective-permute-start(f32[64,640]{1,0:T(8,128)S(1)} %get-tuple-element.77), channel_id=1, source_target_pairs={{0,48},{16,0},{32,16},{48,32},{1,49},{17,1},{33,17},{49,33},{2,50}... | collective-permute-start | bytes 491528 | tf_op jit(solution)/shard_map/ppermute | solution.py:53
  148.2 5.3 %collective-permute-start.4 = (f32[16,640]{1,0:T(8,128)S(1)}, f32[16,640]{1,0:T(8,128)S(1)}, u32[]{:S(2)}, u32[]{:S(2)}) collective-permute-start(f32[16,640]{1,0:T(8,128)S(1)} %get-tuple-element.87), channel_id=1, source_target_pairs={{0,64},{64,128},{128,192},{192,0},{1,65},{65,129},{129,193},{193,1... | collective-permute-start | bytes 122888 | tf_op jit(solution)/shard_map/ppermute | solution.py:53
  149.4 5.5 %collective-permute-start.5 = (f32[16,640]{1,0:T(8,128)S(1)}, f32[16,640]{1,0:T(8,128)S(1)}, u32[]{:S(2)}, u32[]{:S(2)}) collective-permute-start(f32[16,640]{1,0:T(8,128)S(1)} %get-tuple-element.89), channel_id=1, source_target_pairs={{0,128},{64,192},{128,0},{192,64},{1,129},{65,193},{129,1},{193,65... | collective-permute-start | bytes 122888 | tf_op jit(solution)/shard_map/ppermute | solution.py:53
  152.2 4.0 %collective-permute-start.6 = (f32[16,640]{1,0:T(8,128)S(1)}, f32[16,640]{1,0:T(8,128)S(1)}, u32[]{:S(2)}, u32[]{:S(2)}) collective-permute-start(f32[16,640]{1,0:T(8,128)S(1)} %get-tuple-element.88), channel_id=1, source_target_pairs={{0,192},{64,0},{128,64},{192,128},{1,193},{65,1},{129,65},{193,129... | collective-permute-start | bytes 122888 | tf_op jit(solution)/shard_map/ppermute | solution.py:53
Sparse Core Ops, SparseCore 0:
  10.3 43.7 all-gather.1
  74.4 16.0 reduce-scatter.2
  93.0 43.9 reduce-scatter.4
where the time goes:
time: 165 us
  waiting for transfers between devices  59.8 us (36%)
  blocking collectives  34.5 us (21%)
  other arithmetic  19 us (12%)
  between operations  14.2 us (9%)
  local copies, waits for them, and re-layouts  13.6 us (8%)
  matrix products  12.7 us (8%)
  starting transfers between devices  11 us (7%)
    psum x1, blocking collectives, per_device(): vectors = lax.psum(vectors, second_axis)  32 us
    all_gather x1, waiting for transfers between devices, per_device(): lax.all_gather(lax.dynamic_slice_in_dim(both, core * half, half, axis=1),...  31.3 us
    reduce_scatter x1, waiting for transfers between devices, per_device(): lax.psum_scatter(packed, second_axis, scatter_dimension=0, tiled=True)  13.6 us
    ppermute x6, starting transfers between devices, permute_scatter(): lax.ppermute(chunk, axis, [(j, (j + step) % n) for j in range(n)])  10.7 us
    ppermute x6, waiting for transfers between devices, permute_scatter(): lax.ppermute(chunk, axis, [(j, (j + step) % n) for j in range(n)])  7.47 us
    ppermute x1, waiting for transfers between devices, per_device(): other = lax.ppermute(own, 'c', [(0, 1), (1, 0)])  4.49 us
    dot_general x1, matrix products, per_device(): lax.dot_general(jnp.concatenate([conv_lhs, mix_lhs], axis=0), jnp.concate...  4.38 us
    unnamed x17, local copies, waits for them, and re-layouts  4.23 us
  transfers between devices with their start and end apart: 10, of which 8 were waited for; matrix products, arithmetic and copies ran while one was open for 14% of the time, Pallas kernels for 0%

commit v1 on v0

--- a/solution.py
+++ b/solution.py
@@ -64,8 +64,18 @@
     both = jnp.concatenate([conv_weight, mix_weight], axis=0)
     core = lax.axis_index("c")
     half = C // 2
-    own = lax.all_gather(
-        lax.dynamic_slice_in_dim(both, core * half, half, axis=1), "z", axis=0, tiled=True
+    own = jnp.concatenate(
+        jax.lax.all_to_all(
+            jnp.stack(
+                jax.lax.axis_size("z")
+                * [lax.dynamic_slice_in_dim(both, core * half, half, axis=1)],
+                axis=0,
+            ),
+            "z",
+            0,
+            0,
+        ),
+        axis=0,
     )
     audio_f = audio.astype(jnp.float32)
     act_in, slope_in, dalpha_in = snake_parts(audio_f, alpha_in)

time: 165 us -> 179 us (1.085)
  starting transfers between devices: 11 us -> 19.2 us
  waiting for transfers between devices: 59.8 us -> 66.2 us
  other arithmetic: 19 us -> 16.7 us
    all_to_all x0 -> x1, waiting for transfers between devices: none -> 39.4 us  [per_device(): jax.lax.all_to_all(jnp.stack(jax.lax.axis_size('z') * [lax.dynamic_slice_...]
    all_gather x1 -> x0, waiting for transfers between devices: 31.3 us -> none  [per_device(): lax.all_gather(lax.dynamic_slice_in_dim(both, core * half, half, axis=1),...]
    all_to_all x0 -> x1, starting transfers between devices: none -> 8.6 us  [per_device(): jax.lax.all_to_all(jnp.stack(jax.lax.axis_size('z') * [lax.dynamic_slice_...]
    reduce_scatter x1, waiting for transfers between devices: 2.9 us -> 0.61 us  [per_device(): lax.psum_scatter(packed.astype(jnp.bfloat16), first_axis, scatter_dimensi...]
    unnamed x17 -> x19, local copies, waits for them, and re-layouts: 4.23 us -> 3.86 us
  transfers between devices with their start and end apart: 10 -> 10, of which waited for: 8 -> 9; matrix products, arithmetic and copies ran while one was open for 14% -> 12% of each run, Pallas kernels for 0% -> 0%
where the time goes in v1:
time: 179 us
  waiting for transfers between devices  66.2 us (37%)
  blocking collectives  34.4 us (19%)
  starting transfers between devices  19.2 us (11%)
  other arithmetic  16.7 us (9%)
  local copies, waits for them, and re-layouts  14.7 us (8%)
  between operations  14.5 us (8%)
  matrix products  12.8 us (7%)
    all_to_all x1, waiting for transfers between devices, per_device(): jax.lax.all_to_all(jnp.stack(jax.lax.axis_size('z') * [lax.dynamic_slice_...  39.4 us
    psum x1, blocking collectives, per_device(): vectors = lax.psum(vectors, second_axis)  31.9 us
    reduce_scatter x1, waiting for transfers between devices, per_device(): lax.psum_scatter(packed, second_axis, scatter_dimension=0, tiled=True)  13.6 us
    ppermute x6, starting transfers between devices, permute_scatter(): lax.ppermute(chunk, axis, [(j, (j + step) % n) for j in range(n)])  10.3 us
    all_to_all x1, starting transfers between devices, per_device(): jax.lax.all_to_all(jnp.stack(jax.lax.axis_size('z') * [lax.dynamic_slice_...  8.6 us
    ppermute x6, waiting for transfers between devices, permute_scatter(): lax.ppermute(chunk, axis, [(j, (j + step) % n) for j in range(n)])  8.12 us
    ppermute x1, waiting for transfers between devices, per_device(): other = lax.ppermute(own, 'c', [(0, 1), (1, 0)])  4.48 us
    dot_general x1, matrix products, per_device(): lax.dot_general(jnp.concatenate([conv_lhs, mix_lhs], axis=0), jnp.concate...  4.39 us
  transfers between devices with their start and end apart: 10, of which 9 were waited for; matrix products, arithmetic and copies ran while one was open for 12% of the time, Pallas kernels for 0%

profile of v1, /device:TPU:8, one launch (start us, length us, event | category | flops | bytes accessed | tf_op | source)
XLA Modules:
  0.0 178.5 jit_solution(8204874767437501839)
XLA Ops:
  7.2 1.0 fusion.19
  8.1 1.5 stack.12
  9.6 8.6 %all-to-all-start = ((bf16[8,512,256]{2,1,0:T(8,128)(2,1)}), bf16[8,512,256]{2,1,0:T(8,128)(2,1)}, u32[]{:S(2)}, u32[]{:S(2)}) async-start(bf16[8,512,256]{2,1,0:T(8,128)(2,1)} %stack.12), calls=%async_computation | async-start | bytes 4194304 | tf_op jit(solution)/shard_map/all_to_all | solution.py:68
  18.8 1.8 %fusion.10 = bf16[256,512]{1,0:T(8,128)(2,1)S(1)} fusion(bf16[256,512]{1,0:T(8,128)(2,1)S(1)} %copy-done.1, f32[512]{0:T(512)S(1)} %copy-done.5), kind=kLoop, calls=%fused_computation.31 | loop fusion | flops 786432 | bytes 526336 | tf_op jit(solution)/shard_map/convert_element_type | solution.py:82
  21.2 1.8 %constant_dynamic-update-slice_fusion = bf16[256,3584]{1,0:T(8,128)(2,1)S(1)} fusion(bf16[256,3584]{1,0:T(8,128)(2,1)S(1)} %select_dynamic-update-slice_fusion.3, f32[512]{0:T(512)S(1)} %copy-done.5, bf16[256,512]{1,0:T(8,128)(2,1)S(1)} %copy-done.1), kind=kLoop, calls=%fused_computation.72 | loop fusion | flops 786432 | bytes 526336
  23.5 1.3 copy-done.2
  24.8 2.3 %copy.34 = bf16[256,3584]{0,1:T(8,128)(2,1)} copy(bf16[256,3584]{1,0:T(8,128)(2,1)S(1)} %select_dynamic-update-slice_fusion) | data formatting | bytes 3670016 | tf_op jit(solution)/shard_map/concatenate | solution.py:90
  27.1 2.5 %reshape.134 = bf16[256,256,14]{0,2,1:T(8,128)(2,1)S(1)} reshape(bf16[256,3584]{0,1:T(8,128)(2,1)} %copy.34) | data formatting | bytes 3670016 | tf_op jit(solution)/shard_map/reshape | solution.py:105
  30.1 39.4 %all-to-all-done = bf16[8,512,256]{2,1,0:T(8,128)(2,1)} async-done(((bf16[8,512,256]{2,1,0:T(8,128)(2,1)}), bf16[8,512,256]{2,1,0:T(8,128)(2,1)}, u32[]{:S(2)}, u32[]{:S(2)}) %all-to-all-start) | async-done | bytes 2097184 | tf_op jit(solution)/shard_map/all_to_all | solution.py:68
  69.5 4.5 %collective-permute-done = bf16[4096,256]{1,0:T(8,128)(2,1)} collective-permute-done((bf16[4096,256]{1,0:T(8,128)(2,1)}, bf16[4096,256]{1,0:T(8,128)(2,1)}, u32[]{:S(2)}, u32[]{:S(2)}) %collective-permute-start) | collective-permute-done | bytes 2097184 | tf_op jit(solution)/shard_map/ppermute | solution.py:110
  74.0 2.5 %broadcast_select_fusion.1 = (bf16[4096,256]{1,0:T(8,128)(2,1)S(1)}, bf16[4096,256]{1,0:T(8,128)(2,1)S(1)}) fusion(bf16[4096,256]{1,0:T(8,128)(2,1)} %bitcast.2, bf16[4096,256]{1,0:T(8,128)(2,1)} %collective-permute-done, pred[]{:T(512)S(6)} %eq.30), kind=kLoop, calls=%fused_computation.7 | loop fusion | flops 2097152 | bytes 8388609 | tf_op jit(solution)/shard_map/jit(_where)/select_n | solution.py:111
  77.2 1.8 %copy-done.3 = bf16[256,3584]{1,0:T(8,128)(2,1)S(1)} copy-done((bf16[256,3584]{1,0:T(8,128)(2,1)S(1)}, bf16[256,3584]{1,0:T(8,128)(2,1)}, u32[]{:S(2)}) %copy-start.3) | copy-done | bytes 1835032
  79.0 1.1 convolution_add_fusion
  80.1 4.1 %convert_reduce_fusion.1 = (f32[512]{0:T(512)S(1)}, bf16[256,512]{1,0:T(8,128)(2,1)S(1)}, f32[512]{0:T(512)S(1)}, bf16[256,512]{1,0:T(8,128)(2,1)S(1)}) fusion(f32[256,512]{1,0:T(8,128)S(1)} %convolution_add_fusion, f32[512]{0:T(512)S(1)} %get-tuple-element.90, f32[512]{0:T(512)S(1)} %get-tuple-element.91, f32[512]{0:T(512)S(1)} %copy-done.6, ...), kind=kOutput, calls=%fused_computation.42 | convolution fusion | flops 136444928 | bytes 1845248 | tf_op jit(solution)/shard_map/dot_general | solution.py:121
  85.2 4.4 %convolution_convert_fusion = bf16[4096,512]{1,0:T(8,128)(2,1)} fusion(bf16[256,4096]{0,1:T(8,128)(2,1)S(1)} %bitcast.53, bf16[256,4096]{0,1:T(8,128)(2,1)S(1)} %bitcast.52, bf16[256,512]{1,0:T(8,128)(2,1)S(1)} %copy-done.4, bf16[256,512]{1,0:T(8,128)(2,1)S(1)} %get-tuple-element.63), kind=kOutput, calls=%fused_computation | convolution fusion | flops 2159017984 | bytes 8912896 | tf_op jit(solution)/shard_map/dot_general | solution.py:149
  90.1 3.2 %convolution_convert_fusion.1 = bf16[256,3584]{1,0:T(8,128)(2,1)S(1)} fusion(bf16[256,512]{1,0:T(8,128)(2,1)S(1)} %get-tuple-element.63, bf16[3584,512]{1,0:T(8,128)(2,1)} %bitcast.49), kind=kOutput, calls=%fused_computation.1 | convolution fusion | flops 940441600 | bytes 5767168 | tf_op jit(solution)/shard_map/dot_general | solution.py:125
  94.0 3.9 %fusion.18 = (f32[512]{0:T(512)S(1)}, f32[256,512]{1,0:T(8,128)S(1)}) fusion(bf16[256,512]{1,0:T(8,128)(2,1)S(1)} %copy-done.1, f32[512]{0:T(512)S(1)} %get-tuple-element.93, f32[512]{0:T(512)S(1)} %get-tuple-element.92, f32[512]{0:T(512)S(1)} %copy-done.5, f32[229,512]{1,0:T(8,128)S(1)} %get-tuple-element.110, f32[238,512]{1,0:T(8,128)S(1)} %get-tuple-element.108, ...), kind=kLoop, calls=%fused_computation.48 | loop fusion | flops 2227712 | bytes 3981312 | tf_op jit(solution)/shard_map/reduce_sum | solution.py:139
  97.9 2.5 %convert_reduce_fusion = (f32[512]{0:T(512)S(1)}, bf16[256,512]{1,0:T(8,128)(2,1)}) fusion(bf16[256,512]{1,0:T(8,128)(2,1)S(1)} %copy-done.4, f32[256,512]{1,0:T(8,128)S(1)} %get-tuple-element.65, bf16[256,512]{1,0:T(8,128)(2,1)S(1)} %copy-done.1, f32[512]{0:T(512)S(1)} %get-tuple-element.92), kind=kLoop, calls=%fused_computation.22 | loop fusion | flops 1048064 | bytes 1314816 | tf_op jit(solution)/shard_map/reduce_sum | solution.py:138
  100.4 2.5 %psum.14 = f32[4,512]{1,0:T(4,128)S(1)} all-reduce(f32[4,512]{1,0:T(4,128)S(1)} %pad_maximum_fusion.1), channel_id=1, replica_groups=mesh['x'=4,'y'=4,'c'=2,'z'=8] {'c'}, use_global_device_ids=true, to_apply=%region_7.8 | all-reduce | flops 2048 | bytes 16384 | tf_op jit(solution)/shard_map/psum | solution.py:159
  104.2 31.9 %psum.15 = f32[4,4,2,8,8]{3,2,1,0,4:T(2,128)S(1)} all-reduce(f32[4,4,2,8,8]{3,2,1,0,4:T(2,128)S(1)} %reshape.144), channel_id=1, replica_groups=mesh['x'=4,'y'=4,'c'=2,'z'=8] {'z'}, use_global_device_ids=true, to_apply=%region_9.10 | all-reduce | flops 2048 | bytes 16384 | tf_op jit(solution)/shard_map/psum | solution.py:163
  136.5 13.6 %reduce-scatter.5.cloned.1.call-done = bf16[256,512]{1,0:T(8,128)(2,1)} async-done(((bf16[2048,512]{1,0:T(8,128)(2,1)}), bf16[256,512]{1,0:T(8,128)(2,1)}) %reduce-scatter.5.cloned.1.call-update) | async-done | bytes 262160 | tf_op jit(solution)/shard_map/reduce_scatter | solution.py:161
  150.1 1.0 convert_element_type.72
  151.2 1.6 collective-permute-start.1
  152.8 1.2 collective-permute-start.2
  153.9 2.0 %collective-permute-start.3 = (f32[64,640]{1,0:T(8,128)S(1)}, f32[64,640]{1,0:T(8,128)S(1)}, u32[]{:S(2)}, u32[]{:S(2)}) collective-permute-start(f32[64,640]{1,0:T(8,128)S(1)} %get-tuple-element.77), channel_id=1, source_target_pairs={{0,48},{16,0},{32,16},{48,32},{1,49},{17,1},{33,17},{49,33},{2,50}... | collective-permute-start | bytes 491528 | tf_op jit(solution)/shard_map/ppermute | solution.py:53
  156.6 3.1 %collective-permute-done.2 = f32[64,640]{1,0:T(8,128)S(1)} collective-permute-done((f32[64,640]{1,0:T(8,128)S(1)}, f32[64,640]{1,0:T(8,128)S(1)}, u32[]{:S(2)}, u32[]{:S(2)}) %collective-permute-start.2) | collective-permute-done | bytes 163872 | tf_op jit(solution)/shard_map/ppermute | solution.py:53
  159.7 1.3 collective-permute-done.3
  161.1 1.4 collective-permute-start.4
  162.5 3.2 %collective-permute-start.5 = (f32[16,640]{1,0:T(8,128)S(1)}, f32[16,640]{1,0:T(8,128)S(1)}, u32[]{:S(2)}, u32[]{:S(2)}) collective-permute-start(f32[16,640]{1,0:T(8,128)S(1)} %get-tuple-element.89), channel_id=1, source_target_pairs={{0,128},{64,192},{128,0},{192,64},{1,129},{65,193},{129,1},{193,65... | collective-permute-start | bytes 122888 | tf_op jit(solution)/shard_map/ppermute | solution.py:53
  165.7 1.0 collective-permute-start.6
  166.7 1.4 collective-permute-done.5
  168.1 1.6 collective-permute-done.6
  (73 shorter events, 9.0 us)
Async XLA Ops:
  9.6 8.6 %copy-start.8 = (s32[1,8]{1,0:T(1,128)S(1)}, s32[1,8]{1,0:T(1,128)}, u32[]{:S(2)}) copy-start(s32[1,8]{1,0:T(1,128)} %param.12) | copy-start | bytes 100
  9.6 9.2 %copy-start.1 = (bf16[256,512]{1,0:T(8,128)(2,1)S(1)}, bf16[256,512]{1,0:T(8,128)(2,1)}, u32[]{:S(2)}) copy-start(bf16[256,512]{1,0:T(8,128)(2,1)} %param.10) | copy-start | bytes 786436
  9.6 9.2 %copy-start.5 = (f32[512]{0:T(512)S(1)}, f32[512]{0:T(512)}, u32[]{:S(2)}) copy-start(f32[512]{0:T(512)} %param.16) | copy-start | bytes 6148
  9.6 59.9 %all-to-all-start = ((bf16[8,512,256]{2,1,0:T(8,128)(2,1)}), bf16[8,512,256]{2,1,0:T(8,128)(2,1)}, u32[]{:S(2)}, u32[]{:S(2)}) async-start(bf16[8,512,256]{2,1,0:T(8,128)(2,1)} %stack.12), calls=%async_computation | async-start | bytes 4194304 | tf_op jit(solution)/shard_map/all_to_all | solution.py:68
  18.2 85.3 %reduce-scatter.3.cloned.1.call-start = ((), (), s32[]{:S(2)}) async-start(), calls=%async_computation.3 | async-start | bytes 6291456 | tf_op jit(solution)/shard_map/reduce_scatter | solution.py:156
  23.5 1.3 copy-start.2
  29.8 39.7 %copy-start.6 = (f32[512]{0:T(512)S(1)}, f32[512]{0:T(512)}, u32[]{:S(2)}) copy-start(f32[512]{0:T(512)} %param.17) | copy-start | bytes 6148
  69.5 4.5 %collective-permute-start = (bf16[4096,256]{1,0:T(8,128)(2,1)}, bf16[4096,256]{1,0:T(8,128)(2,1)}, u32[]{:S(2)}, u32[]{:S(2)}) collective-permute-start(bf16[4096,256]{1,0:T(8,128)(2,1)} %bitcast.2), channel_id=1, source_target_pairs={{0,8},{8,0},{1,9},{9,1},{2,10},{10,2},{3,11},{11,3},{4,12},{12,4},... | collective-permute-start | bytes 6291464 | tf_op jit(solution)/shard_map/ppermute | solution.py:110
  76.8 2.2 %copy-start.3 = (bf16[256,3584]{1,0:T(8,128)(2,1)S(1)}, bf16[256,3584]{1,0:T(8,128)(2,1)}, u32[]{:S(2)}) copy-start(bf16[256,3584]{1,0:T(8,128)(2,1)} %copy-done.2) | copy-start | bytes 5505028
  76.9 2.2 %copy-start.7 = (f32[512]{0:T(512)S(1)}, f32[512]{0:T(512)}, u32[]{:S(2)}) copy-start(f32[512]{0:T(512)} %param.15) | copy-start | bytes 6148
  77.1 3.0 %copy-start = (bf16[8,448,512]{2,1,0:T(8,128)(2,1)}, bf16[8,448,512]{2,1,0:T(8,128)(2,1)S(1)}, u32[]{:S(2)}) copy-start(bf16[8,448,512]{2,1,0:T(8,128)(2,1)S(1)} %slice.174) | copy-start | bytes 11010052
  79.0 1.1 copy-start.4
  89.7 60.4 %reduce-scatter.5.cloned.1.call-start = ((), (), s32[]{:S(2)}) async-start(), calls=%async_computation.4 | async-start | bytes 2359296 | tf_op jit(solution)/shard_map/reduce_scatter | solution.py:161
  151.2 5.4 %collective-permute-start.1 = (f32[64,640]{1,0:T(8,128)S(1)}, f32[64,640]{1,0:T(8,128)S(1)}, u32[]{:S(2)}, u32[]{:S(2)}) collective-permute-start(f32[64,640]{1,0:T(8,128)S(1)} %get-tuple-element.75), channel_id=1, source_target_pairs={{0,16},{16,32},{32,48},{48,0},{1,17},{17,33},{33,49},{49,1},{2,18}... | collective-permute-start | bytes 491528 | tf_op jit(solution)/shard_map/ppermute | solution.py:53
  152.8 6.9 %collective-permute-start.2 = (f32[64,640]{1,0:T(8,128)S(1)}, f32[64,640]{1,0:T(8,128)S(1)}, u32[]{:S(2)}, u32[]{:S(2)}) collective-permute-start(f32[64,640]{1,0:T(8,128)S(1)} %get-tuple-element.76), channel_id=1, source_target_pairs={{0,32},{16,48},{32,0},{48,16},{1,33},{17,49},{33,1},{49,17},{2,34}... | collective-permute-start | bytes 491528 | tf_op jit(solution)/shard_map/ppermute | solution.py:53
  153.9 7.1 %collective-permute-start.3 = (f32[64,640]{1,0:T(8,128)S(1)}, f32[64,640]{1,0:T(8,128)S(1)}, u32[]{:S(2)}, u32[]{:S(2)}) collective-permute-start(f32[64,640]{1,0:T(8,128)S(1)} %get-tuple-element.77), channel_id=1, source_target_pairs={{0,48},{16,0},{32,16},{48,32},{1,49},{17,1},{33,17},{49,33},{2,50}... | collective-permute-start | bytes 491528 | tf_op jit(solution)/shard_map/ppermute | solution.py:53
  161.1 5.6 %collective-permute-start.4 = (f32[16,640]{1,0:T(8,128)S(1)}, f32[16,640]{1,0:T(8,128)S(1)}, u32[]{:S(2)}, u32[]{:S(2)}) collective-permute-start(f32[16,640]{1,0:T(8,128)S(1)} %get-tuple-element.87), channel_id=1, source_target_pairs={{0,64},{64,128},{128,192},{192,0},{1,65},{65,129},{129,193},{193,1... | collective-permute-start | bytes 122888 | tf_op jit(solution)/shard_map/ppermute | solution.py:53
  162.5 5.7 %collective-permute-start.5 = (f32[16,640]{1,0:T(8,128)S(1)}, f32[16,640]{1,0:T(8,128)S(1)}, u32[]{:S(2)}, u32[]{:S(2)}) collective-permute-start(f32[16,640]{1,0:T(8,128)S(1)} %get-tuple-element.89), channel_id=1, source_target_pairs={{0,128},{64,192},{128,0},{192,64},{1,129},{65,193},{129,1},{193,65... | collective-permute-start | bytes 122888 | tf_op jit(solution)/shard_map/ppermute | solution.py:53
  165.7 4.0 %collective-permute-start.6 = (f32[16,640]{1,0:T(8,128)S(1)}, f32[16,640]{1,0:T(8,128)S(1)}, u32[]{:S(2)}, u32[]{:S(2)}) collective-permute-start(f32[16,640]{1,0:T(8,128)S(1)} %get-tuple-element.88), channel_id=1, source_target_pairs={{0,192},{64,0},{128,64},{192,128},{1,193},{65,1},{129,65},{193,129... | collective-permute-start | bytes 122888 | tf_op jit(solution)/shard_map/ppermute | solution.py:53
Sparse Core Ops, SparseCore 0:
  89.8 13.7 reduce-scatter.2
  106.1 43.9 reduce-scatter.4
